TPU v7x, 512 devices: a whole 4x8x8 slice. The times are simulated.
512 devices in a mesh: rows: 32 (over x, y_hi, core), cols: 16 (over z, y_lo).
Axes of the slice: x: 4, y: 8 (y_hi: 4, y_lo: 2; y = y_hi * 2 + y_lo), z: 8, core: 2. Of those that a mesh axis runs over, the one named last changes fastest.
Arguments:
- greens: bfloat16 [512, 262144], P('cols', 'rows'), may hold values from -0.5 to 0.5
- slip_values: bfloat16 [8192, 128], P('cols'), may hold values from 0.5 to 4
- rupture_ids: int32 [8192, 128], P('cols'), may hold values from -1 to 511, as said below
- win_point: int32 [4096], P('rows'), may hold values from 0 to 1023, never falling along the last dimension, each value on 1 to 32 neighbouring positions
Outputs:
- window_peak: float32 [8192, 4096], P('cols', 'rows')
Inputs may be any that keep to these rules, and one draw needn't show every extreme that they name: `rupture_ids`: each row lists its sources as one run of consecutive source numbers in its first slots and -1 in the rest; some row fills all 128 slots. `win_point`: never falls along the windows; every point holds 1 to 32 consecutive windows and some point exactly 32.
All inputs are finite; a program needn't handle non-finite values.
Results may differ from a plain program's by a relative error of at most 0.0003.
Values may be sent and summed in bfloat16 or wider, within the bound.
No kernel may reach another device: no remote copies, remote signals or barrier semaphores. Data moves between devices by JAX's collectives and lax.ppermute only.
A program may use at most 64 MiB of HBM per device.

v0:
```python
import jax
import jax.numpy as jnp
from jax import lax
from jax.sharding import Mesh
from jax.sharding import PartitionSpec as P

TSTEP = 64
COLS = ("cols_0", "cols_1")
SPLIT = "cols_0"
SHARE = "cols_1"


def extended(cells, sides, width):
    for axis, dim in sides:
        count = lax.axis_size(axis)
        ends = count - 1
        head = lax.slice_in_dim(cells, 0, width, axis=dim)
        tail = lax.slice_in_dim(cells, cells.shape[dim] - width, cells.shape[dim], axis=dim)
        cells = jnp.concatenate(
            [
                lax.ppermute(tail, axis, [(i, (i + 1) % count) for i in range(ends)]),
                cells,
                lax.ppermute(head, axis, [((i + 1) % count, i) for i in range(ends)]),
            ],
            axis=dim,
        )
    return cells


def shifted_slips(values, starts, width):
    count, slots = values.shape
    dense = jnp.concatenate([values, jnp.zeros((count, width - slots), values.dtype)], axis=1)
    bits = max(1, (width - 1).bit_length())
    for bit in range(bits):
        step = 1 << bit
        rolled = jnp.concatenate([dense[:, width - step :], dense[:, : width - step]], axis=1)
        dense = jnp.where((starts >> bit & 1)[:, None] == 1, rolled, dense)
    return dense


def combine(earlier, later):
    flag = jnp.logical_or(earlier[0], later[0])
    value = jnp.where(later[0], later[1], jnp.maximum(earlier[1], later[1]))
    return (flag, value)


def point_peaks(window_max, win_point):
    windows = window_max.shape[1]
    begins = jnp.concatenate([jnp.ones((1,), bool), win_point[1:] != win_point[:-1]])
    finals = jnp.concatenate([win_point[:-1] != win_point[1:], jnp.ones((1,), bool)])
    begin_flags = jnp.broadcast_to(begins[None, :], window_max.shape)
    final_flags = jnp.broadcast_to(finals[None, :], window_max.shape)
    forward = lax.associative_scan(combine, (begin_flags, window_max), axis=1)[1]
    backward = lax.associative_scan(combine, (final_flags, window_max), reverse=True, axis=1)[1]
    local_peak = jnp.maximum(forward, backward)
    edge_values = jnp.stack([backward[:, 0], forward[:, windows - 1]], axis=1)
    edge_points = jnp.stack([win_point[0] + 1, win_point[windows - 1] + 1]).astype(jnp.float32)[
        None, :
    ]
    padded_values, padded_points = (
        extended(edge_values, (("rows", 1),), 1),
        extended(edge_points, (("rows", 1),), 1),
    )
    point_code = (win_point + 1).astype(jnp.float32)[None, :]
    from_left = jnp.maximum(local_peak, padded_values[:, 0:1])
    local_peak = jnp.where(point_code == padded_points[0, 0], from_left, local_peak)
    from_right = jnp.maximum(local_peak, padded_values[:, 3:4])
    local_peak = jnp.where(point_code == padded_points[0, 3], from_right, local_peak)
    return local_peak


def local(greens, slip_values, rupture_ids, win_point):
    parts = lax.axis_size(SPLIT)
    shares = lax.axis_size(SHARE)
    own_sources, rows = greens.shape
    width = own_sources * parts * shares
    scen = slip_values.shape[0]
    block = rows // parts
    listed = rupture_ids >= 0
    values = jnp.where(listed, slip_values, jnp.zeros_like(slip_values))
    starts = jnp.maximum(rupture_ids[:, 0], 0)
    all_values = lax.all_gather(values, SPLIT, axis=0, tiled=True)
    all_starts = lax.all_gather(starts, SPLIT, axis=0, tiled=True)
    pieces = greens.reshape(own_sources, parts, block)
    pieces = lax.all_to_all(pieces, SPLIT, 1, 0, tiled=True)
    pieces = pieces.reshape(parts, own_sources, block)
    pieces = lax.all_gather(pieces, SHARE, axis=0, tiled=False)
    panel_t = jnp.transpose(pieces, (3, 1, 0, 2)).reshape(block, width)
    dense = shifted_slips(all_values, all_starts, width)
    wave_t = lax.dot_general(
        panel_t, dense, (((1,), (1,)), ((), ())), preferred_element_type=jnp.float32
    )
    win_block = block // TSTEP
    maxima = jnp.max(wave_t.reshape(win_block, TSTEP, parts * scen), axis=1)
    maxima = maxima.reshape(win_block, parts, scen)
    maxima = lax.all_to_all(maxima, SPLIT, 1, 0, tiled=True)
    window_max = maxima.reshape(parts * win_block, scen).T
    return point_peaks(window_max, win_point)


def solution(mesh):
    split = Mesh(mesh.devices.reshape(mesh.shape["rows"], 8, 2), ("rows", "cols_0", "cols_1"))
    in_specs = (P(COLS, "rows"), P(COLS, None), P(COLS, None), P("rows"))
    out_specs = P(COLS, "rows")
    return jax.shard_map(local, mesh=split, in_specs=in_specs, out_specs=out_specs, check_vma=False)
```

profile of v0, /device:TPU:21, one launch (start us, length us, event | category | flops | bytes accessed | tf_op | source)
XLA Modules:
  0.0 163.6 jit_solution(4431919119020084951)
XLA Ops:
  6.5 1.7 %compare_select_fusion = bf16[512,128]{1,0:T(8,128)(2,1)} fusion(bf16[512,128]{1,0:T(8,128)(2,1)} %param.5, s32[512,128]{1,0:T(8,128)} %param.6), kind=kLoop, calls=%fused_computation.38 | loop fusion | flops 131072 | bytes 524288 | tf_op jit(solution)/shard_map/jit(_where)/select_n | solution.py:80
  8.3 1.9 %copy.27 = bf16[4,8,8,1024]{3,2,0,1:T(8,128)(2,1)} copy(bf16[4,8,8,1024]{3,2,1,0:T(8,128)(2,1)} %bitcast.57) | data formatting | bytes 1048576 | tf_op jit(solution)/shard_map/reshape | solution.py:84
  10.2 10.0 %all-to-all-start = ((bf16[32,8,1024]{2,0,1:T(8,128)(2,1)}), bf16[32,8,1024]{2,0,1:T(8,128)(2,1)S(1)}, u32[]{:S(2)}, u32[]{:S(2)}) async-start(bf16[32,8,1024]{2,0,1:T(8,128)(2,1)} %bitcast.35), calls=%async_computation | async-start | bytes 1048576 | tf_op jit(solution)/shard_map/all_to_all | solution.py:85
  20.3 1.3 fusion.22
  22.8 1.0 slice_maximum_fusion
  23.8 40.5 %all-gather = s32[4096,1]{1,0:T(8,128)S(1)} all-gather(s32[512,1]{1,0:T(8,128)S(1)} %slice_maximum_fusion), channel_id=2, replica_groups=mesh['rows'=32,'cols_0'=8,'cols_1'=2] {'cols_0'}, dimensions={0}, use_global_device_ids=true | all-gather | bytes 18432 | tf_op jit(solution)/shard_map/all_gather | solution.py:83
  64.4 5.1 %fusion.4 = (pred[4096]{0:T(1024)(128)(4,1)S(1)}, pred[4096]{0:T(1024)(128)(4,1)S(1)}, pred[4096]{0:T(1024)(128)(4,1)S(1)}, pred[4096]{0:T(1024)(128)(4,1)S(1)},...) fusion(s32[4096,1]{1,0:T(8,128)S(1)} %all-gather), kind=kLoop, calls=%fused_computation.24 | loop fusion | flops 110592 | bytes 53248 | tf_op jit(solution)/shard_map/eq | solution.py:37
  69.4 0.8 copy-done.2
  70.3 1.7 %pad_slice_fusion = bf16[4096,511]{1,0:T(8,128)(2,1)S(1)} fusion(bf16[4096,128]{1,0:T(8,128)(2,1)} %all-gather.5.cloned.1.call-done), kind=kLoop, calls=%fused_computation.2 | loop fusion | bytes 5234688 | tf_op jit(solution)/shard_map/slice | solution.py:36
  72.0 4.1 %pad_select_fusion = bf16[4096,512]{1,0:T(8,128)(2,1)S(1)} fusion(bf16[4096,128]{1,0:T(8,128)(2,1)S(1)} %copy-done.1, bf16[4096,511]{1,0:T(8,128)(2,1)S(1)} %pad_slice_fusion, pred[4096]{0:T(1024)(128)(4,1)S(1)} %get-tuple-element.13), kind=kLoop, calls=%fused_computation.1 | loop fusion | flops 2097152 | bytes 9433088 | tf_op jit(solution)/shard_map/jit(_where)/select_n | solution.py:37
  76.4 4.0 %maximum_select_fusion = bf16[4096,512]{1,0:T(8,128)(2,1)S(1)} fusion(bf16[4096,512]{1,0:T(8,128)(2,1)S(1)} %pad_select_fusion, bf16[4096,510]{1,0:T(8,128)(2,1)S(1)} %bitcast.43, bf16[4096,2]{1,0:T(8,128)(2,1)S(1)} %slice.575, pred[4096]{0:T(1024)(128)(4,1)S(1)} %get-tuple-element.6), kind=kLoop, calls=%fused_computation.3 | loop fusion | flops 10485760 | bytes 12587008 | tf_op jit(solution)/shard_map/jit(_where)/select_n | solution.py:37
  80.8 4.0 %maximum_select_fusion.1 = bf16[4096,512]{1,0:T(8,128)(2,1)S(1)} fusion(bf16[4096,512]{1,0:T(8,128)(2,1)S(1)} %maximum_select_fusion, bf16[4096,508]{1,0:T(8,128)(2,1)S(1)} %bitcast.44, bf16[4096,4]{1,0:T(8,128)(2,1)S(1)} %slice.577, pred[4096]{0:T(1024)(128)(4,1)S(1)} %get-tuple-element.7), kind=kLoop, calls=%fused_computation.4 | loop fusion | flops 10485760 | bytes 12587008 | tf_op jit(solution)/shard_map/jit(_where)/select_n | solution.py:37
  85.2 4.0 %maximum_select_fusion.2 = bf16[4096,512]{1,0:T(8,128)(2,1)S(1)} fusion(bf16[4096,512]{1,0:T(8,128)(2,1)S(1)} %maximum_select_fusion.1, bf16[4096,504]{1,0:T(8,128)(2,1)S(1)} %bitcast.45, bf16[4096,8]{1,0:T(8,128)(2,1)S(1)} %slice.579, pred[4096]{0:T(1024)(128)(4,1)S(1)} %get-tuple-element.8), kind=kLoop, calls=%fused_computation.5 | loop fusion | flops 10485760 | bytes 12587008 | tf_op jit(solution)/shard_map/jit(_where)/select_n | solution.py:37
  89.6 4.0 %maximum_select_fusion.3 = bf16[4096,512]{1,0:T(8,128)(2,1)S(1)} fusion(bf16[4096,512]{1,0:T(8,128)(2,1)S(1)} %maximum_select_fusion.2, bf16[4096,496]{1,0:T(8,128)(2,1)S(1)} %bitcast.46, bf16[4096,16]{1,0:T(8,128)(2,1)S(1)} %slice.581, pred[4096]{0:T(1024)(128)(4,1)S(1)} %get-tuple-element.9), kind=kLoop, calls=%fused_computation.6 | loop fusion | flops 10485760 | bytes 12587008 | tf_op jit(solution)/shard_map/jit(_where)/select_n | solution.py:37
  94.0 4.0 %maximum_select_fusion.4 = bf16[4096,512]{1,0:T(8,128)(2,1)S(1)} fusion(bf16[4096,512]{1,0:T(8,128)(2,1)S(1)} %maximum_select_fusion.3, bf16[4096,480]{1,0:T(8,128)(2,1)S(1)} %bitcast.47, bf16[4096,32]{1,0:T(8,128)(2,1)S(1)} %slice.583, pred[4096]{0:T(1024)(128)(4,1)S(1)} %get-tuple-element.10), kind=kLoop, calls=%fused_computation.7 | loop fusion | flops 10485760 | bytes 12587008 | tf_op jit(solution)/shard_map/jit(_where)/select_n | solution.py:37
  98.4 4.2 %maximum_select_fusion.5 = bf16[4096,512]{1,0:T(8,128)(2,1)S(1)} fusion(bf16[4096,512]{1,0:T(8,128)(2,1)S(1)} %maximum_select_fusion.4, bf16[4096,448]{1,0:T(8,128)(2,1)S(1)} %bitcast.48, bf16[4096,64]{1,0:T(8,128)(2,1)S(1)} %slice.585, pred[4096]{0:T(1024)(128)(4,1)S(1)} %get-tuple-element.11), kind=kLoop, calls=%fused_computation.8 | loop fusion | flops 10485760 | bytes 12587008 | tf_op jit(solution)/shard_map/jit(_where)/select_n | solution.py:37
  103.1 2.2 %maximum_select_fusion.6 = bf16[4096,512]{1,0:T(8,128)(2,1)S(1)} fusion(bf16[4096,512]{1,0:T(8,128)(2,1)S(1)} %maximum_select_fusion.5, bf16[4096,384]{1,0:T(8,128)(2,1)S(1)} %slice.588, bf16[4096,128]{1,0:T(8,128)(2,1)S(1)} %slice.587, pred[4096]{0:T(1024)(128)(4,1)S(1)} %get-tuple-element.12), kind=kLoop, calls=%fused_computation.9 | loop fusion | flops 10485760 | bytes 12587008 | tf_op jit(solution)/shard_map/jit(_where)/select_n | solution.py:37
  105.4 1.9 %copy-done = bf16[4096,512]{1,0:T(8,128)(2,1)} copy-done((bf16[4096,512]{1,0:T(8,128)(2,1)}, bf16[4096,512]{1,0:T(8,128)(2,1)S(1)}, u32[]{:S(2)}) %copy-start) | copy-done | bytes 4194328
  107.3 1.6 fusion.17
  108.9 1.3 copy.20
  110.2 7.0 %bitcast_reduce_fusion = f32[16,4096]{1,0:T(8,128)S(1)} fusion(bf16[1024,512]{0,1:T(8,128)(2,1)S(1)} %bitcast.56, bf16[4096,512]{1,0:T(8,128)(2,1)} %copy-done, bf16[4096,256]{1,0:T(8,128)(2,1)} %get-tuple-element.15, bf16[4096,256]{1,0:T(8,128)(2,1)S(1)} %get-tuple-element.14, pred[4096]{0:T(1024)(128)(4,1)S(1)} %get-tuple-element.5), kind=kOutput, calls=%fused_computation | convolution fusion | flops 4309581824 | bytes 9703424 | tf_op jit(solution)/shard_map/dot_general | solution.py:90
  117.2 0.7 copy.28
  118.0 5.1 %all-to-all-start.1 = ((f32[16,8,512]{2,0,1:T(8,128)}), f32[16,8,512]{2,0,1:T(8,128)S(1)}, u32[]{:S(2)}, u32[]{:S(2)}) async-start(f32[16,8,512]{2,0,1:T(8,128)} %bitcast.36), calls=%async_computation.1 | async-start | bytes 524288 | tf_op jit(solution)/shard_map/all_to_all | solution.py:96
  123.6 7.0 %collective-permute-start = (f32[1,1]{1,0:T(1,128)}, f32[1,1]{1,0:T(1,128)}, u32[]{:S(2)}, u32[]{:S(2)}) collective-permute-start(f32[1,1]{1,0:T(1,128)} %get-tuple-element.28), channel_id=1, source_target_pairs={{16,0},{32,16},{48,32},{64,48},{80,64},{96,80},{112,96},{128,112},... | collective-permute-start | bytes 20 | tf_op jit(solution)/shard_map/ppermute | solution.py:23
  130.6 5.1 %collective-permute-start.1 = (f32[1,1]{1,0:T(1,128)}, f32[1,1]{1,0:T(1,128)}, u32[]{:S(2)}, u32[]{:S(2)}) collective-permute-start(f32[1,1]{1,0:T(1,128)} %get-tuple-element.29), channel_id=1, source_target_pairs={{0,16},{16,32},{32,48},{48,64},{64,80},{80,96},{96,112},{112,128},... | collective-permute-start | bytes 20 | tf_op jit(solution)/shard_map/ppermute | solution.py:21
  137.4 0.6 slice.501
  143.4 0.6 broadcast_select_fusion
  145.5 2.6 %collective-permute-start.2 = (f32[512,1]{0,1:T(1,128)S(1)}, f32[512,1]{0,1:T(1,128)S(1)}, u32[]{:S(2)}, u32[]{:S(2)}) collective-permute-start(f32[512,1]{0,1:T(1,128)S(1)} %slice_add_fusion.1), channel_id=1, source_target_pairs={{0,16},{16,32},{32,48},{48,64},{64,80},{80,96},{96,112},{112,128},... | collective-permute-start | bytes 6152 | tf_op jit(solution)/shard_map/ppermute | solution.py:21
  148.8 1.9 %collective-permute-start.3 = (f32[512,1]{0,1:T(1,128)S(1)}, f32[512,1]{0,1:T(1,128)S(1)}, u32[]{:S(2)}, u32[]{:S(2)}) collective-permute-start(f32[512,1]{0,1:T(1,128)S(1)} %slice_add_fusion), channel_id=1, source_target_pairs={{16,0},{32,16},{48,32},{64,48},{80,64},{96,80},{112,96},{128,112},... | collective-permute-start | bytes 6152 | tf_op jit(solution)/shard_map/ppermute | solution.py:23
  150.8 1.3 convert_compare_fusion.1
  152.3 3.6 %collective-permute-done.3 = f32[512,1]{0,1:T(1,128)S(1)} collective-permute-done((f32[512,1]{0,1:T(1,128)S(1)}, f32[512,1]{0,1:T(1,128)S(1)}, u32[]{:S(2)}, u32[]{:S(2)}) %collective-permute-start.3) | collective-permute-done | bytes 2080 | tf_op jit(solution)/shard_map/ppermute | solution.py:23
  156.0 0.8 copy.22
  (204 shorter events, 12.2 us)
Async XLA Ops:
  6.5 63.7 %all-gather.5.cloned.1.call-start = ((), (), s32[]{:S(2)}) async-start(), calls=%async_computation.2 | async-start | bytes 1179648 | tf_op jit(solution)/shard_map/all_gather | solution.py:82
  10.2 59.3 %all-to-all-start = ((bf16[32,8,1024]{2,0,1:T(8,128)(2,1)}), bf16[32,8,1024]{2,0,1:T(8,128)(2,1)S(1)}, u32[]{:S(2)}, u32[]{:S(2)}) async-start(bf16[32,8,1024]{2,0,1:T(8,128)(2,1)} %bitcast.35), calls=%async_computation | async-start | bytes 1048576 | tf_op jit(solution)/shard_map/all_to_all | solution.py:85
  20.2 88.7 %all-gather.7.cloned.1.call-start = ((), (), s32[]{:S(2)}) async-start(), calls=%async_computation.3 | async-start | bytes 1572864 | tf_op jit(solution)/shard_map/all_gather | solution.py:87
  69.4 0.8 copy-start.2
  70.3 1.7 %copy-start.1 = (bf16[4096,128]{1,0:T(8,128)(2,1)S(1)}, bf16[4096,128]{1,0:T(8,128)(2,1)}, u32[]{:S(2)}) copy-start(bf16[4096,128]{1,0:T(8,128)(2,1)} %all-gather.5.cloned.1.call-done) | copy-start | bytes 3145732
  105.4 1.9 %copy-start = (bf16[4096,512]{1,0:T(8,128)(2,1)}, bf16[4096,512]{1,0:T(8,128)(2,1)S(1)}, u32[]{:S(2)}) copy-start(bf16[4096,512]{1,0:T(8,128)(2,1)S(1)} %maximum_select_fusion.6) | copy-start | bytes 12582916
  110.2 25.6 %copy-start.3 = (s32[128]{0:T(128)S(1)}, s32[128]{0:T(128)}, u32[]{:S(2)}) copy-start(s32[128]{0:T(128)} %param.7) | copy-start | bytes 1540
  118.0 23.2 %all-to-all-start.1 = ((f32[16,8,512]{2,0,1:T(8,128)}), f32[16,8,512]{2,0,1:T(8,128)S(1)}, u32[]{:S(2)}, u32[]{:S(2)}) async-start(f32[16,8,512]{2,0,1:T(8,128)} %bitcast.36), calls=%async_computation.1 | async-start | bytes 524288 | tf_op jit(solution)/shard_map/all_to_all | solution.py:96
  123.6 27.2 %collective-permute-start = (f32[1,1]{1,0:T(1,128)}, f32[1,1]{1,0:T(1,128)}, u32[]{:S(2)}, u32[]{:S(2)}) collective-permute-start(f32[1,1]{1,0:T(1,128)} %get-tuple-element.28), channel_id=1, source_target_pairs={{16,0},{32,16},{48,32},{64,48},{80,64},{96,80},{112,96},{128,112},... | collective-permute-start | bytes 20 | tf_op jit(solution)/shard_map/ppermute | solution.py:23
  130.6 20.1 %collective-permute-start.1 = (f32[1,1]{1,0:T(1,128)}, f32[1,1]{1,0:T(1,128)}, u32[]{:S(2)}, u32[]{:S(2)}) collective-permute-start(f32[1,1]{1,0:T(1,128)} %get-tuple-element.29), channel_id=1, source_target_pairs={{0,16},{16,32},{32,48},{48,64},{64,80},{80,96},{96,112},{112,128},... | collective-permute-start | bytes 20 | tf_op jit(solution)/shard_map/ppermute | solution.py:21
  145.5 6.8 %collective-permute-start.2 = (f32[512,1]{0,1:T(1,128)S(1)}, f32[512,1]{0,1:T(1,128)S(1)}, u32[]{:S(2)}, u32[]{:S(2)}) collective-permute-start(f32[512,1]{0,1:T(1,128)S(1)} %slice_add_fusion.1), channel_id=1, source_target_pairs={{0,16},{16,32},{32,48},{48,64},{64,80},{80,96},{96,112},{112,128},... | collective-permute-start | bytes 6152 | tf_op jit(solution)/shard_map/ppermute | solution.py:21
  148.8 7.0 %collective-permute-start.3 = (f32[512,1]{0,1:T(1,128)S(1)}, f32[512,1]{0,1:T(1,128)S(1)}, u32[]{:S(2)}, u32[]{:S(2)}) collective-permute-start(f32[512,1]{0,1:T(1,128)S(1)} %slice_add_fusion), channel_id=1, source_target_pairs={{16,0},{32,16},{48,32},{64,48},{80,64},{96,80},{112,96},{128,112},... | collective-permute-start | bytes 6152 | tf_op jit(solution)/shard_map/ppermute | solution.py:23
Sparse Core Ops, SparseCore 0:
  9.4 47.3 all-gather.4
  70.4 32.4 all-gather.6
where the time goes:
time: 164 us
  other arithmetic  42.9 us (26%)
  blocking collectives  40.5 us (25%)
  starting transfers between devices  31.8 us (19%)
  local copies, waits for them, and re-layouts  22.3 us (14%)
  between operations  15.6 us (10%)
  matrix products  6.99 us (4%)
  waiting for transfers between devices  3.65 us (2%)
    all_gather x1, blocking collectives, local(): all_starts = lax.all_gather(starts, SPLIT, axis=0, tiled=True)  40.5 us
    select_n x8, other arithmetic, shifted_slips(): dense = jnp.where((starts >> bit & 1)[:, None] == 1, rolled, dense)  30.8 us
    all_to_all x1, starting transfers between devices, local(): pieces = lax.all_to_all(pieces, SPLIT, 1, 0, tiled=True)  10 us
    ppermute x2, starting transfers between devices, extended(): lax.ppermute(head, axis, [((i + 1) % count, i) for i in range(ends)])  8.94 us
    ppermute x2, starting transfers between devices, extended(): lax.ppermute(tail, axis, [(i, (i + 1) % count) for i in range(ends)])  7.7 us
    dot_general x1, matrix products, local(): lax.dot_general(panel_t, dense, (((1,), (1,)), ((), ())), preferred_eleme...  6.99 us
    eq x1, other arithmetic, shifted_slips(): dense = jnp.where((starts >> bit & 1)[:, None] == 1, rolled, dense)  5.06 us
    all_to_all x1, starting transfers between devices, local(): maxima = lax.all_to_all(maxima, SPLIT, 1, 0, tiled=True)  5.05 us
  transfers between devices with their start and end apart: 8, of which 1 were waited for; matrix products, arithmetic and copies ran while one was open for 35% of the time, Pallas kernels for 0%

commit v1 on v0

--- a/solution.py
+++ b/solution.py
@@ -80,7 +80,9 @@
     values = jnp.where(listed, slip_values, jnp.zeros_like(slip_values))
     starts = jnp.maximum(rupture_ids[:, 0], 0)
     all_values = lax.all_gather(values, SPLIT, axis=0, tiled=True)
-    all_starts = lax.all_gather(starts, SPLIT, axis=0, tiled=True)
+    all_starts = jnp.concatenate(
+        lax.all_to_all(jnp.stack([starts] * lax.axis_size(SPLIT)), SPLIT, 0, 0), axis=0
+    )
     pieces = greens.reshape(own_sources, parts, block)
     pieces = lax.all_to_all(pieces, SPLIT, 1, 0, tiled=True)
     pieces = pieces.reshape(parts, own_sources, block)

time: 164 us -> 149 us (0.909)
  the two profiles are of different devices: /device:TPU:21 before, /device:TPU:23 now
where the time goes in v1:
time: 149 us; the launch traced here: 148 us
  other arithmetic  38.3 us (26%)
  starting transfers between devices  33.7 us (23%)
  waiting for transfers between devices  30.4 us (20%)
  local copies, waits for them, and re-layouts  23 us (15%)
  between operations  15.6 us (10%)
  matrix products  7.17 us (5%)
    select_n x8, other arithmetic, shifted_slips(): dense = jnp.where((starts >> bit & 1)[:, None] == 1, rolled, dense)  30.6 us
    all_to_all x1, waiting for transfers between devices, local(): pieces = lax.all_to_all(pieces, SPLIT, 1, 0, tiled=True)  17.4 us
    all_to_all x1, starting transfers between devices, local(): lax.all_to_all(jnp.stack([starts] * lax.axis_size(SPLIT)), SPLIT, 0, 0)  10 us
    ppermute x2, starting transfers between devices, extended(): lax.ppermute(head, axis, [((i + 1) % count, i) for i in range(ends)])  7.91 us
    ppermute x2, starting transfers between devices, extended(): lax.ppermute(tail, axis, [(i, (i + 1) % count) for i in range(ends)])  7.69 us
    dot_general x1, matrix products, local(): lax.dot_general(panel_t, dense, (((1,), (1,)), ((), ())), preferred_eleme...  7.17 us
    all_to_all x1, waiting for transfers between devices, local(): lax.all_to_all(jnp.stack([starts] * lax.axis_size(SPLIT)), SPLIT, 0, 0)  4.72 us
    all_gather x1, waiting for transfers between devices, local(): all_values = lax.all_gather(values, SPLIT, axis=0, tiled=True)  4.62 us
  transfers between devices with their start and end apart: 9, of which 4 were waited for; matrix products, arithmetic and copies ran while one was open for 36% of the time, Pallas kernels for 0%

profile of v1, /device:TPU:23, one launch (start us, length us, event | category | flops | bytes accessed | tf_op | source)
XLA Modules:
  0.0 148.1 jit_solution(9590646941835409951)
XLA Ops:
  6.5 1.7 %compare_select_fusion = bf16[512,128]{1,0:T(8,128)(2,1)} fusion(bf16[512,128]{1,0:T(8,128)(2,1)} %param.5, s32[512,128]{1,0:T(8,128)} %param.6), kind=kLoop, calls=%fused_computation.20 | loop fusion | flops 131072 | bytes 524288 | tf_op jit(solution)/shard_map/jit(_where)/select_n | solution.py:80
  8.3 1.1 maximum_reduce_fusion
  10.0 10.0 %all-to-all-start = ((s32[8,1,512]{2,1,0:T(1,128)}), s32[8,1,512]{2,1,0:T(1,128)S(1)}, u32[]{:S(2)}, u32[]{:S(2)}) async-start(s32[8,1,512]{2,1,0:T(1,128)} %stack.11), calls=%async_computation | async-start | bytes 32768 | tf_op jit(solution)/shard_map/all_to_all | solution.py:84
  20.0 1.9 %copy.36 = bf16[4,8,8,1024]{3,2,0,1:T(8,128)(2,1)} copy(bf16[4,8,8,1024]{3,2,1,0:T(8,128)(2,1)} %bitcast.75) | data formatting | bytes 1048576 | tf_op jit(solution)/shard_map/reshape | solution.py:86
  21.9 4.7 %all-to-all-done = s32[8,1,512]{2,1,0:T(1,128)S(1)} async-done(((s32[8,1,512]{2,1,0:T(1,128)}), s32[8,1,512]{2,1,0:T(1,128)S(1)}, u32[]{:S(2)}, u32[]{:S(2)}) %all-to-all-start) | async-done | bytes 16416 | tf_op jit(solution)/shard_map/all_to_all | solution.py:84
  26.6 3.5 %all-to-all-start.1 = ((bf16[32,8,1024]{2,0,1:T(8,128)(2,1)}), bf16[32,8,1024]{2,0,1:T(8,128)(2,1)S(1)}, u32[]{:S(2)}, u32[]{:S(2)}) async-start(bf16[32,8,1024]{2,0,1:T(8,128)(2,1)} %bitcast.53), calls=%async_computation.1 | async-start | bytes 1048576 | tf_op jit(solution)/shard_map/all_to_all | solution.py:87
  30.2 1.3 fusion.13
  33.5 17.4 %all-to-all-done.1 = bf16[32,8,1024]{2,0,1:T(8,128)(2,1)S(1)} async-done(((bf16[32,8,1024]{2,0,1:T(8,128)(2,1)}), bf16[32,8,1024]{2,0,1:T(8,128)(2,1)S(1)}, u32[]{:S(2)}, u32[]{:S(2)}) %all-to-all-start.1) | async-done | bytes 524320 | tf_op jit(solution)/shard_map/all_to_all | solution.py:87
  50.9 0.8 copy-done.2
  51.7 4.6 %all-gather.4.cloned.1.call-done = bf16[4096,128]{1,0:T(8,128)(2,1)} async-done(((bf16[512,128]{1,0:T(8,128)(2,1)}), bf16[4096,128]{1,0:T(8,128)(2,1)}) %all-gather.4.cloned.1.call-update) | async-done | bytes 1048592 | tf_op jit(solution)/shard_map/all_gather | solution.py:82
  56.3 1.7 %pad_slice_fusion = bf16[4096,511]{1,0:T(8,128)(2,1)S(1)} fusion(bf16[4096,128]{1,0:T(8,128)(2,1)} %all-gather.4.cloned.1.call-done), kind=kLoop, calls=%fused_computation.2 | loop fusion | bytes 5234688 | tf_op jit(solution)/shard_map/slice | solution.py:36
  58.0 4.1 %pad_select_fusion = bf16[4096,512]{1,0:T(8,128)(2,1)S(1)} fusion(bf16[4096,128]{1,0:T(8,128)(2,1)S(1)} %copy-done.1, bf16[4096,511]{1,0:T(8,128)(2,1)S(1)} %pad_slice_fusion, pred[4096]{0:T(1024)(128)(4,1)S(1)} %bitcast.84), kind=kLoop, calls=%fused_computation.1 | loop fusion | flops 2097152 | bytes 9433088 | tf_op jit(solution)/shard_map/jit(_where)/select_n | solution.py:37
  62.5 4.0 %maximum_select_fusion = bf16[4096,512]{1,0:T(8,128)(2,1)S(1)} fusion(bf16[4096,512]{1,0:T(8,128)(2,1)S(1)} %pad_select_fusion, bf16[4096,510]{1,0:T(8,128)(2,1)S(1)} %bitcast.61, bf16[4096,2]{1,0:T(8,128)(2,1)S(1)} %slice.575, pred[4096]{0:T(1024)(128)(4,1)S(1)} %bitcast.82), kind=kLoop, calls=%fused_computation.3 | loop fusion | flops 10485760 | bytes 12587008 | tf_op jit(solution)/shard_map/jit(_where)/select_n | solution.py:37
  66.9 4.0 %maximum_select_fusion.1 = bf16[4096,512]{1,0:T(8,128)(2,1)S(1)} fusion(bf16[4096,512]{1,0:T(8,128)(2,1)S(1)} %maximum_select_fusion, bf16[4096,508]{1,0:T(8,128)(2,1)S(1)} %bitcast.62, bf16[4096,4]{1,0:T(8,128)(2,1)S(1)} %slice.577, pred[4096]{0:T(1024)(128)(4,1)S(1)} %bitcast.81), kind=kLoop, calls=%fused_computation.4 | loop fusion | flops 10485760 | bytes 12587008 | tf_op jit(solution)/shard_map/jit(_where)/select_n | solution.py:37
  71.3 4.0 %maximum_select_fusion.2 = bf16[4096,512]{1,0:T(8,128)(2,1)S(1)} fusion(bf16[4096,512]{1,0:T(8,128)(2,1)S(1)} %maximum_select_fusion.1, bf16[4096,504]{1,0:T(8,128)(2,1)S(1)} %bitcast.63, bf16[4096,8]{1,0:T(8,128)(2,1)S(1)} %slice.579, pred[4096]{0:T(1024)(128)(4,1)S(1)} %bitcast.80), kind=kLoop, calls=%fused_computation.5 | loop fusion | flops 10485760 | bytes 12587008 | tf_op jit(solution)/shard_map/jit(_where)/select_n | solution.py:37
  75.7 4.0 %maximum_select_fusion.3 = bf16[4096,512]{1,0:T(8,128)(2,1)S(1)} fusion(bf16[4096,512]{1,0:T(8,128)(2,1)S(1)} %maximum_select_fusion.2, bf16[4096,496]{1,0:T(8,128)(2,1)S(1)} %bitcast.64, bf16[4096,16]{1,0:T(8,128)(2,1)S(1)} %slice.581, pred[4096]{0:T(1024)(128)(4,1)S(1)} %bitcast.79), kind=kLoop, calls=%fused_computation.6 | loop fusion | flops 10485760 | bytes 12587008 | tf_op jit(solution)/shard_map/jit(_where)/select_n | solution.py:37
  80.1 4.0 %maximum_select_fusion.4 = bf16[4096,512]{1,0:T(8,128)(2,1)S(1)} fusion(bf16[4096,512]{1,0:T(8,128)(2,1)S(1)} %maximum_select_fusion.3, bf16[4096,480]{1,0:T(8,128)(2,1)S(1)} %bitcast.65, bf16[4096,32]{1,0:T(8,128)(2,1)S(1)} %slice.583, pred[4096]{0:T(1024)(128)(4,1)S(1)} %bitcast.78), kind=kLoop, calls=%fused_computation.7 | loop fusion | flops 10485760 | bytes 12587008 | tf_op jit(solution)/shard_map/jit(_where)/select_n | solution.py:37
  84.5 4.0 %maximum_select_fusion.5 = bf16[4096,512]{1,0:T(8,128)(2,1)S(1)} fusion(bf16[4096,512]{1,0:T(8,128)(2,1)S(1)} %maximum_select_fusion.4, bf16[4096,448]{1,0:T(8,128)(2,1)S(1)} %bitcast.66, bf16[4096,64]{1,0:T(8,128)(2,1)S(1)} %slice.585, pred[4096]{0:T(1024)(128)(4,1)S(1)} %bitcast.77), kind=kLoop, calls=%fused_computation.8 | loop fusion | flops 10485760 | bytes 12587008 | tf_op jit(solution)/shard_map/jit(_where)/select_n | solution.py:37
  89.0 2.2 %maximum_select_fusion.6 = bf16[4096,512]{1,0:T(8,128)(2,1)S(1)} fusion(bf16[4096,512]{1,0:T(8,128)(2,1)S(1)} %maximum_select_fusion.5, bf16[4096,384]{1,0:T(8,128)(2,1)S(1)} %slice.588, bf16[4096,128]{1,0:T(8,128)(2,1)S(1)} %slice.587, pred[4096]{0:T(1024)(128)(4,1)S(1)} %bitcast.83), kind=kLoop, calls=%fused_computation.9 | loop fusion | flops 10485760 | bytes 12587008 | tf_op jit(solution)/shard_map/jit(_where)/select_n | solution.py:37
  91.3 1.9 %copy-done = bf16[4096,512]{1,0:T(8,128)(2,1)} copy-done((bf16[4096,512]{1,0:T(8,128)(2,1)}, bf16[4096,512]{1,0:T(8,128)(2,1)S(1)}, u32[]{:S(2)}) %copy-start) | copy-done | bytes 4194328
  93.2 1.6 %fusion.8 = (bf16[4096,256]{1,0:T(8,128)(2,1)S(1)}, bf16[4096,256]{1,0:T(8,128)(2,1)}) fusion(bf16[4096,512]{1,0:T(8,128)(2,1)S(1)} %maximum_select_fusion.6), kind=kLoop, calls=%fused_computation.87 | loop fusion | bytes 8388608 | tf_op jit(solution)/shard_map/slice | solution.py:36
  94.8 1.3 copy.20
  96.1 7.2 %bitcast_reduce_fusion = f32[16,4096]{1,0:T(8,128)S(1)} fusion(bf16[1024,512]{0,1:T(8,128)(2,1)S(1)} %bitcast.74, bf16[4096,512]{1,0:T(8,128)(2,1)} %copy-done, bf16[4096,256]{1,0:T(8,128)(2,1)} %get-tuple-element.15, bf16[4096,256]{1,0:T(8,128)(2,1)S(1)} %get-tuple-element.14, pred[4096]{0:T(1024)(128)(4,1)S(1)} %bitcast.94), kind=kOutput, calls=%fused_computation | convolution fusion | flops 4309581824 | bytes 9703424 | tf_op jit(solution)/shard_map/dot_general | solution.py:92
  103.3 0.7 copy.37
  104.0 4.5 %all-to-all-start.2 = ((f32[16,8,512]{2,0,1:T(8,128)}), f32[16,8,512]{2,0,1:T(8,128)S(1)}, u32[]{:S(2)}, u32[]{:S(2)}) async-start(f32[16,8,512]{2,0,1:T(8,128)} %bitcast.54), calls=%async_computation.2 | async-start | bytes 524288 | tf_op jit(solution)/shard_map/all_to_all | solution.py:98
  109.1 6.0 %collective-permute-start = (f32[1,1]{1,0:T(1,128)}, f32[1,1]{1,0:T(1,128)}, u32[]{:S(2)}, u32[]{:S(2)}) collective-permute-start(f32[1,1]{1,0:T(1,128)} %get-tuple-element.28), channel_id=1, source_target_pairs={{16,0},{32,16},{48,32},{64,48},{80,64},{96,80},{112,96},{128,112},... | collective-permute-start | bytes 20 | tf_op jit(solution)/shard_map/ppermute | solution.py:23
  115.1 5.1 %collective-permute-start.1 = (f32[1,1]{1,0:T(1,128)}, f32[1,1]{1,0:T(1,128)}, u32[]{:S(2)}, u32[]{:S(2)}) collective-permute-start(f32[1,1]{1,0:T(1,128)} %get-tuple-element.29), channel_id=1, source_target_pairs={{0,16},{16,32},{32,48},{48,64},{64,80},{80,96},{96,112},{112,128},... | collective-permute-start | bytes 20 | tf_op jit(solution)/shard_map/ppermute | solution.py:21
  129.9 2.6 %collective-permute-start.2 = (f32[512,1]{0,1:T(1,128)S(1)}, f32[512,1]{0,1:T(1,128)S(1)}, u32[]{:S(2)}, u32[]{:S(2)}) collective-permute-start(f32[512,1]{0,1:T(1,128)S(1)} %slice_add_fusion.1), channel_id=1, source_target_pairs={{0,16},{16,32},{32,48},{48,64},{64,80},{80,96},{96,112},{112,128},... | collective-permute-start | bytes 6152 | tf_op jit(solution)/shard_map/ppermute | solution.py:21
  133.3 1.9 %collective-permute-start.3 = (f32[512,1]{0,1:T(1,128)S(1)}, f32[512,1]{0,1:T(1,128)S(1)}, u32[]{:S(2)}, u32[]{:S(2)}) collective-permute-start(f32[512,1]{0,1:T(1,128)S(1)} %slice_add_fusion), channel_id=1, source_target_pairs={{16,0},{32,16},{48,32},{64,48},{80,64},{96,80},{112,96},{128,112},... | collective-permute-start | bytes 6152 | tf_op jit(solution)/shard_map/ppermute | solution.py:23
  135.2 1.3 convert_compare_fusion.1
  136.7 3.6 %collective-permute-done.3 = f32[512,1]{0,1:T(1,128)S(1)} collective-permute-done((f32[512,1]{0,1:T(1,128)S(1)}, f32[512,1]{0,1:T(1,128)S(1)}, u32[]{:S(2)}, u32[]{:S(2)}) %collective-permute-start.3) | collective-permute-done | bytes 2080 | tf_op jit(solution)/shard_map/ppermute | solution.py:23
  140.4 0.8 copy.22
  (215 shorter events, 14.6 us)
Async XLA Ops:
  6.5 49.8 %all-gather.4.cloned.1.call-start = ((), (), s32[]{:S(2)}) async-start(), calls=%async_computation.3 | async-start | bytes 1179648 | tf_op jit(solution)/shard_map/all_gather | solution.py:82
  10.0 16.7 %all-to-all-start = ((s32[8,1,512]{2,1,0:T(1,128)}), s32[8,1,512]{2,1,0:T(1,128)S(1)}, u32[]{:S(2)}, u32[]{:S(2)}) async-start(s32[8,1,512]{2,1,0:T(1,128)} %stack.11), calls=%async_computation | async-start | bytes 32768 | tf_op jit(solution)/shard_map/all_to_all | solution.py:84
  26.6 24.3 %all-to-all-start.1 = ((bf16[32,8,1024]{2,0,1:T(8,128)(2,1)}), bf16[32,8,1024]{2,0,1:T(8,128)(2,1)S(1)}, u32[]{:S(2)}, u32[]{:S(2)}) async-start(bf16[32,8,1024]{2,0,1:T(8,128)(2,1)} %bitcast.53), calls=%async_computation.1 | async-start | bytes 1048576 | tf_op jit(solution)/shard_map/all_to_all | solution.py:87
  30.1 64.6 %all-gather.6.cloned.1.call-start = ((), (), s32[]{:S(2)}) async-start(), calls=%async_computation.4 | async-start | bytes 1572864 | tf_op jit(solution)/shard_map/all_gather | solution.py:89
  50.9 0.8 copy-start.2
  56.3 1.7 %copy-start.1 = (bf16[4096,128]{1,0:T(8,128)(2,1)S(1)}, bf16[4096,128]{1,0:T(8,128)(2,1)}, u32[]{:S(2)}) copy-start(bf16[4096,128]{1,0:T(8,128)(2,1)} %all-gather.4.cloned.1.call-done) | copy-start | bytes 3145732
  91.3 1.9 %copy-start = (bf16[4096,512]{1,0:T(8,128)(2,1)}, bf16[4096,512]{1,0:T(8,128)(2,1)S(1)}, u32[]{:S(2)}) copy-start(bf16[4096,512]{1,0:T(8,128)(2,1)S(1)} %maximum_select_fusion.6) | copy-start | bytes 12582916
  96.1 24.1 %copy-start.3 = (s32[128]{0:T(128)S(1)}, s32[128]{0:T(128)}, u32[]{:S(2)}) copy-start(s32[128]{0:T(128)} %param.7) | copy-start | bytes 1540
  104.0 21.6 %all-to-all-start.2 = ((f32[16,8,512]{2,0,1:T(8,128)}), f32[16,8,512]{2,0,1:T(8,128)S(1)}, u32[]{:S(2)}, u32[]{:S(2)}) async-start(f32[16,8,512]{2,0,1:T(8,128)} %bitcast.54), calls=%async_computation.2 | async-start | bytes 524288 | tf_op jit(solution)/shard_map/all_to_all | solution.py:98
  109.1 26.1 %collective-permute-start = (f32[1,1]{1,0:T(1,128)}, f32[1,1]{1,0:T(1,128)}, u32[]{:S(2)}, u32[]{:S(2)}) collective-permute-start(f32[1,1]{1,0:T(1,128)} %get-tuple-element.28), channel_id=1, source_target_pairs={{16,0},{32,16},{48,32},{64,48},{80,64},{96,80},{112,96},{128,112},... | collective-permute-start | bytes 20 | tf_op jit(solution)/shard_map/ppermute | solution.py:23
  115.1 20.1 %collective-permute-start.1 = (f32[1,1]{1,0:T(1,128)}, f32[1,1]{1,0:T(1,128)}, u32[]{:S(2)}, u32[]{:S(2)}) collective-permute-start(f32[1,1]{1,0:T(1,128)} %get-tuple-element.29), channel_id=1, source_target_pairs={{0,16},{16,32},{32,48},{48,64},{64,80},{80,96},{96,112},{112,128},... | collective-permute-start | bytes 20 | tf_op jit(solution)/shard_map/ppermute | solution.py:21
  129.9 6.8 %collective-permute-start.2 = (f32[512,1]{0,1:T(1,128)S(1)}, f32[512,1]{0,1:T(1,128)S(1)}, u32[]{:S(2)}, u32[]{:S(2)}) collective-permute-start(f32[512,1]{0,1:T(1,128)S(1)} %slice_add_fusion.1), channel_id=1, source_target_pairs={{0,16},{16,32},{32,48},{48,64},{64,80},{80,96},{96,112},{112,128},... | collective-permute-start | bytes 6152 | tf_op jit(solution)/shard_map/ppermute | solution.py:21
  133.3 7.0 %collective-permute-start.3 = (f32[512,1]{0,1:T(1,128)S(1)}, f32[512,1]{0,1:T(1,128)S(1)}, u32[]{:S(2)}, u32[]{:S(2)}) collective-permute-start(f32[512,1]{0,1:T(1,128)S(1)} %slice_add_fusion), channel_id=1, source_target_pairs={{16,0},{32,16},{48,32},{64,48},{80,64},{96,80},{112,96},{128,112},... | collective-permute-start | bytes 6152 | tf_op jit(solution)/shard_map/ppermute | solution.py:23
Sparse Core Ops, SparseCore 0:
  9.4 46.8 all-gather.3
  58.4 30.7 all-gather.5
